TPU v7x, 512 devices: a whole 4x8x8 slice. The times are simulated.
512 devices in a mesh: head: 16 (over y, core), seq: 32 (over z, x).
Axes of the slice: x: 4, y: 8, z: 8, core: 2. Of those that a mesh axis runs over, the one named last changes fastest.
Arguments:
- queries: bfloat16 [32768, 2048], P(('seq', 'head'))
- keys: bfloat16 [32768, 2048], P(('seq', 'head'))
- values: bfloat16 [32768, 2048], P(('seq', 'head')), may hold values from -6 to 6
- grad_out: bfloat16 [32768, 2048], P(('seq', 'head')), may hold values from -6 to 6
- random_blocks: int32 [256, 3], P('seq'), may hold values from 0 to 255, as said below
Outputs:
- attended: bfloat16 [32768, 2048], P(('seq', 'head'))
- grad_queries: bfloat16 [32768, 2048], P(('seq', 'head'))
- grad_keys: bfloat16 [32768, 2048], P(('seq', 'head'))
- grad_values: bfloat16 [32768, 2048], P(('seq', 'head'))
Inputs may be any that keep to these rules, and one draw needn't show every extreme that they name: `random_blocks`: within the rows of one sequence group (8 consecutive query blocks), at most 2 entries name blocks of any one group's range of 8 blocks, and in every group's rows one group's range is named exactly 2 times.
All inputs are finite; a program needn't handle non-finite values.
Results may differ from a plain program's by a relative error of at most 0.022.
Values may be sent and summed in bfloat16 or wider, within the bound.
No kernel may reach another device: no remote copies, remote signals or barrier semaphores. Data moves between devices by JAX's collectives and lax.ppermute only.
A program may use at most 192 MiB of HBM per device.

v0:
```python
import jax
import jax.numpy as jnp
from jax import lax
from jax.sharding import PartitionSpec as P

HD = 128
BLK = 128
RAND = 3


def with_halo(cells, sides, width):
    for axis, dim in sides:
        count = lax.axis_size(axis)
        ends = count - 1
        head = lax.slice_in_dim(cells, 0, width, axis=dim)
        tail = lax.slice_in_dim(cells, cells.shape[dim] - width, cells.shape[dim], axis=dim)
        cells = jnp.concatenate(
            [
                lax.ppermute(tail, axis, [(i, (i + 1) % count) for i in range(ends)]),
                cells,
                lax.ppermute(head, axis, [((i + 1) % count, i) for i in range(ends)]),
            ],
            axis=dim,
        )
    return cells


def broadcast(value, axis, source):
    kept = jnp.where(lax.axis_index(axis) == source, value, 0).astype(value.dtype)
    return lax.psum(kept, axis)


def slot_places(owners, groups, capacity):
    owner_hits = (owners[:, None] == jnp.arange(groups, dtype=jnp.int32)[None, :]).astype(jnp.int32)
    earlier = jnp.cumsum(owner_hits, axis=0) - owner_hits
    return owners * capacity + jnp.sum(earlier * owner_hits, axis=1)


def request_table(list_rows, query_count, groups, capacity):
    flat_rows = list_rows.reshape(-1)
    places = slot_places(flat_rows // query_count, groups, capacity)
    matches = places[None, :] == jnp.arange(groups * capacity, dtype=jnp.int32)[:, None]
    table = jnp.sum(jnp.where(matches, (flat_rows % query_count)[None, :], 0), axis=1)
    return table.reshape(groups, capacity)


def window_valid(my_group, query_count, groups):
    block_ids = jnp.arange(query_count, dtype=jnp.int32)
    left_ok = jnp.logical_not(jnp.logical_and(my_group == 0, block_ids == 0))
    right_ok = jnp.logical_not(
        jnp.logical_and(my_group == groups - 1, block_ids == query_count - 1)
    )
    all_true = jnp.ones((query_count, BLK), dtype=bool)
    return jnp.concatenate(
        [
            all_true,
            all_true,
            left_ok[:, None] & all_true,
            all_true,
            right_ok[:, None] & all_true,
            jnp.ones((query_count, RAND * BLK), dtype=bool),
        ],
        axis=1,
    )


def against_keys(rows, global_part, window_part, remote_part):
    return jnp.concatenate(
        [
            jnp.einsum("qihd,jhd->qhij", rows, global_part, preferred_element_type=jnp.float32),
            jnp.einsum("qihd,qjhd->qhij", rows, window_part, preferred_element_type=jnp.float32),
            jnp.einsum("qihd,qjhd->qhij", rows, remote_part, preferred_element_type=jnp.float32),
        ],
        axis=-1,
    )


def split_keys(table):
    return (table[..., : 2 * BLK], table[..., 2 * BLK : 5 * BLK], table[..., 5 * BLK :])


def weigh_keys(table, global_part, window_part, remote_part):
    global_w, window_w, random_w = split_keys(table)
    return (
        jnp.einsum("qhij,jhd->qihd", global_w, global_part, preferred_element_type=jnp.float32)
        + jnp.einsum("qhij,qjhd->qihd", window_w, window_part, preferred_element_type=jnp.float32)
        + jnp.einsum("qhij,qjhd->qihd", random_w, remote_part, preferred_element_type=jnp.float32)
    )


def key_terms(table, rows):
    global_w, window_w, random_w = split_keys(table)
    return (
        jnp.einsum("qhij,qihd->jhd", global_w, rows, preferred_element_type=jnp.float32),
        jnp.einsum("qhij,qihd->qjhd", window_w, rows, preferred_element_type=jnp.float32),
        jnp.einsum("qhij,qihd->qjhd", random_w, rows, preferred_element_type=jnp.float32),
    )


def shards(queries, keys, values, grad_out, random_blocks):
    groups = lax.axis_size("seq")
    my_group = lax.axis_index("seq")
    head_q, head_k, head_v, head_g = (
        lax.all_to_all(queries, "head", split_axis=1, concat_axis=0, tiled=True),
        lax.all_to_all(keys, "head", split_axis=1, concat_axis=0, tiled=True),
        lax.all_to_all(values, "head", split_axis=1, concat_axis=0, tiled=True),
        lax.all_to_all(grad_out, "head", split_axis=1, concat_axis=0, tiled=True),
    )
    group_tokens = head_q.shape[0]
    head_count = head_q.shape[1] // HD
    query_count = group_tokens // BLK
    capacity = max(2, 3 * query_count * RAND // (2 * groups))
    score_scale = HD ** (-0.5)
    key_value = jnp.stack([head_k, head_v])
    kv_blocks = key_value.reshape(2, query_count, BLK, head_count, HD)
    edged = with_halo(key_value, (("seq", 1),), BLK)
    edged = edged.reshape(2, query_count + 2, BLK, head_count, HD)
    window_kv = jnp.concatenate(
        [edged[:, 0:query_count], edged[:, 1 : query_count + 1], edged[:, 2 : query_count + 2]],
        axis=2,
    )
    global_kv = broadcast(kv_blocks[:, 0:2].reshape(2, 2 * BLK, head_count, HD), "seq", 0)
    flat_ids = random_blocks.reshape(-1)
    places = slot_places(flat_ids // query_count, groups, capacity)
    wanted = lax.all_to_all(
        request_table(random_blocks, query_count, groups, capacity),
        "seq",
        split_axis=0,
        concat_axis=0,
        tiled=True,
    )
    served = jnp.take(kv_blocks, wanted.reshape(-1), axis=1)
    served = served.reshape(2, groups, capacity, BLK, head_count, HD)
    fetched = lax.all_to_all(served, "seq", split_axis=1, concat_axis=1, tiled=True)
    chosen = jnp.take(fetched.reshape(2, groups * capacity, BLK, head_count, HD), places, axis=1)
    remote_kv = chosen.reshape(2, query_count, RAND * BLK, head_count, HD)
    query_blocks = head_q.reshape(query_count, BLK, head_count, HD)
    grad_blocks = head_g.reshape(query_count, BLK, head_count, HD)
    scores = score_scale * against_keys(query_blocks, global_kv[0], window_kv[0], remote_kv[0])
    valid = window_valid(my_group, query_count, groups)
    scores = jnp.where(valid[:, None, None, :], scores, -jnp.inf)
    row_max = jnp.max(scores, axis=-1, keepdims=True)
    exponent = jnp.exp(scores - row_max)
    attention_probs = exponent / jnp.sum(exponent, axis=-1, keepdims=True)
    weights = attention_probs.astype(jnp.bfloat16)
    attended = weigh_keys(weights, global_kv[1], window_kv[1], remote_kv[1]).astype(jnp.bfloat16)
    grad_prob = against_keys(grad_blocks, global_kv[1], window_kv[1], remote_kv[1])
    row_delta = jnp.sum(attention_probs * grad_prob, axis=-1, keepdims=True)
    grad_score = (score_scale * attention_probs * (grad_prob - row_delta)).astype(jnp.bfloat16)
    grad_q = weigh_keys(grad_score, global_kv[0], window_kv[0], remote_kv[0]).astype(jnp.bfloat16)
    key_global, key_window, key_random = key_terms(grad_score, query_blocks)
    value_global, value_window, value_random = key_terms(weights, grad_blocks)
    global_sum = lax.psum(jnp.stack([key_global, value_global]).astype(jnp.bfloat16), "seq").astype(
        jnp.float32
    )
    window_grad = jnp.stack([key_window, value_window]).reshape(
        2, query_count, 3, BLK, head_count, HD
    )
    no_pad = (0, 0)
    extended = (
        jnp.pad(window_grad[:, :, 0], (no_pad, (0, 2), no_pad, no_pad, no_pad))
        + jnp.pad(window_grad[:, :, 1], (no_pad, (1, 1), no_pad, no_pad, no_pad))
        + jnp.pad(window_grad[:, :, 2], (no_pad, (2, 0), no_pad, no_pad, no_pad))
    )
    outward = jnp.concatenate([extended[:, 0], extended[:, query_count + 1]], axis=1)
    inward = with_halo(outward.astype(jnp.bfloat16), (("seq", 1),), BLK).astype(outward.dtype)
    own_grad = extended[:, 1 : query_count + 1]
    own_grad = own_grad.at[:, 0].add(inward[:, :BLK])
    own_grad = own_grad.at[:, query_count - 1].add(inward[:, 3 * BLK :])
    random_terms = (
        jnp.stack([key_random, value_random])
        .reshape(2, query_count * RAND, BLK, head_count, HD)
        .astype(jnp.bfloat16)
    )
    send_pick = (places[None, :] == jnp.arange(groups * capacity, dtype=jnp.int32)[:, None]).astype(
        jnp.bfloat16
    )
    outgoing = jnp.einsum(
        "pj,xjihd->xpihd", send_pick, random_terms, preferred_element_type=jnp.float32
    ).astype(jnp.bfloat16)
    incoming = lax.all_to_all(
        outgoing.reshape(2, groups, capacity, BLK, head_count, HD),
        "seq",
        split_axis=1,
        concat_axis=1,
        tiled=True,
    )
    take_pick = (
        wanted.reshape(-1)[None, :] == jnp.arange(query_count, dtype=jnp.int32)[:, None]
    ).astype(jnp.bfloat16)
    random_sum = jnp.einsum(
        "qp,xpihd->xqihd",
        take_pick,
        incoming.reshape(2, groups * capacity, BLK, head_count, HD),
        preferred_element_type=jnp.float32,
    )
    global_sum = global_sum.reshape(2, 2, BLK, head_count, HD)
    own_grad = own_grad.at[:, 0:2].add(jnp.where(my_group == 0, global_sum, 0.0))
    total_grad = own_grad + random_sum
    grad_k = total_grad[0].reshape(group_tokens, head_count * HD).astype(jnp.bfloat16)
    grad_v = total_grad[1].reshape(group_tokens, head_count * HD).astype(jnp.bfloat16)
    return (
        lax.all_to_all(
            attended.reshape(group_tokens, head_count * HD),
            "head",
            split_axis=0,
            concat_axis=1,
            tiled=True,
        ),
        lax.all_to_all(
            grad_q.reshape(group_tokens, head_count * HD),
            "head",
            split_axis=0,
            concat_axis=1,
            tiled=True,
        ),
        lax.all_to_all(grad_k, "head", split_axis=0, concat_axis=1, tiled=True),
        lax.all_to_all(grad_v, "head", split_axis=0, concat_axis=1, tiled=True),
    )


def solution(mesh):
    placed = (
        P(("seq", "head"), None),
        P(("seq", "head"), None),
        P(("seq", "head"), None),
        P(("seq", "head"), None),
        P("seq", None),
    )
    return jax.shard_map(
        shards,
        mesh=mesh,
        in_specs=placed,
        out_specs=(
            P(("seq", "head"), None),
            P(("seq", "head"), None),
            P(("seq", "head"), None),
            P(("seq", "head"), None),
        ),
        check_vma=False,
    )
```

profile of v0, /device:TPU:1, one launch (start us, length us, event | category | flops | bytes accessed | tf_op | source)
XLA Modules:
  0.0 558.6 jit_solution(16468300619809350168)
XLA Ops:
  7.2 0.8 copy.165
  9.3 13.7 %all-to-all-start.3 = ((s32[32,1,2]{2,1,0:T(1,128)}), s32[32,1,2]{2,1,0:T(1,128)S(1)}, u32[]{:S(2)}, u32[]{:S(2)}) async-start(s32[32,1,2]{2,1,0:T(1,128)} %bitcast.20), calls=%async_computation.3 | async-start | bytes 32768 | tf_op jit(solution)/shard_map/all_to_all | solution.py:125
  23.0 0.8 copy_bitcast_fusion.8
  23.8 7.7 %all-to-all-done.3 = s32[32,1,2]{2,1,0:T(1,128)S(1)} async-done(((s32[32,1,2]{2,1,0:T(1,128)}), s32[32,1,2]{2,1,0:T(1,128)S(1)}, u32[]{:S(2)}, u32[]{:S(2)}) %all-to-all-start.3) | async-done | bytes 288 | tf_op jit(solution)/shard_map/all_to_all | solution.py:125
  31.5 9.2 %all-to-all-start.2 = ((bf16[64,16,128]{2,0,1:T(8,128)(2,1)}), bf16[64,16,128]{2,0,1:T(8,128)(2,1)S(1)}, u32[]{:S(2)}, u32[]{:S(2)}) async-start(bf16[64,16,128]{2,0,1:T(8,128)(2,1)} %copy_bitcast_fusion.8), calls=%async_computation.2 | async-start | bytes 524288 | tf_op jit(solution)/shard_map/all_to_all | solution.py:104
  40.7 1.7 copy_bitcast_fusion.10
  42.4 10.0 %all-to-all-done.2 = bf16[64,16,128]{2,0,1:T(8,128)(2,1)S(1)} async-done(((bf16[64,16,128]{2,0,1:T(8,128)(2,1)}), bf16[64,16,128]{2,0,1:T(8,128)(2,1)S(1)}, u32[]{:S(2)}, u32[]{:S(2)}) %all-to-all-start.2) | async-done | bytes 262176 | tf_op jit(solution)/shard_map/all_to_all | solution.py:104
  52.4 3.4 all-to-all-start
  55.9 0.8 copy_bitcast_fusion.9
  56.6 0.8 copy_bitcast_fusion.7
  58.8 8.2 %all-to-all-done = bf16[64,16,128]{2,0,1:T(8,128)(2,1)S(1)} async-done(((bf16[64,16,128]{2,0,1:T(8,128)(2,1)}), bf16[64,16,128]{2,0,1:T(8,128)(2,1)S(1)}, u32[]{:S(2)}, u32[]{:S(2)}) %all-to-all-start) | async-done | bytes 262176 | tf_op jit(solution)/shard_map/all_to_all | solution.py:105
  67.0 3.4 all-to-all-start.1
  70.6 11.6 %all-to-all-done.1 = bf16[64,16,128]{2,0,1:T(8,128)(2,1)S(1)} async-done(((bf16[64,16,128]{2,0,1:T(8,128)(2,1)}), bf16[64,16,128]{2,0,1:T(8,128)(2,1)S(1)}, u32[]{:S(2)}, u32[]{:S(2)}) %all-to-all-start.1) | async-done | bytes 262176 | tf_op jit(solution)/shard_map/all_to_all | solution.py:106
  82.1 3.4 all-to-all-start.6
  85.6 3.0 gather_fusion
  88.7 2.7 copy.169
  91.9 2.5 copy.170
  94.4 2.3 all-to-all-done.6
  96.7 4.9 all-to-all-start.4
  101.9 3.0 collective-permute-start
  104.9 1.5 collective-permute-start.1
  107.0 7.4 %collective-permute-done = bf16[2,128,128]{2,1,0:T(8,128)(2,1)S(1)} collective-permute-done((bf16[2,128,128]{2,1,0:T(8,128)(2,1)S(1)}, bf16[2,128,128]{2,1,0:T(8,128)(2,1)S(1)}, u32[]{:S(2)}, u32[]{:S(2)}) %collective-permute-start) | collective-permute-done | bytes 65568 | tf_op jit(solution)/shard_map/ppermute | solution.py:19
  115.4 0.8 copy-done.6
  116.2 1.5 convolution_bitcast_fusion.1
  117.7 159.4 %all-reduce.6.cloned.1.call-done = bf16[2,256,1,128]{3,1,2,0:T(8,128)(2,1)} async-done(((bf16[2,256,1,128]{3,1,2,0:T(8,128)(2,1)}), bf16[2,256,1,128]{3,1,2,0:T(8,128)(2,1)}) %all-reduce.6.cloned.1.call-update) | async-done | bytes 131088 | tf_op jit(solution)/shard_map/psum | solution.py:30
  277.1 1.1 convolution_bitcast_fusion.6
  278.2 2.1 convolution_bitcast_fusion.5
  280.4 4.8 copy.171
  285.2 4.1 gather_fusion.1
  289.3 1.6 bitcast_select_fusion
  291.5 1.4 fusion.20
  292.9 1.5 fusion.2
  294.8 1.0 copy-done.8
  296.1 1.9 multiply_reduce_fusion
  298.0 2.3 multiply_convert_fusion
  302.9 1.4 convolution_convert_fusion
  304.3 6.7 %copy.190 = bf16[2,32,2,128,1,128]{5,2,3,0,4,1:T(2,128)(2,1)} copy(bf16[2,32,2,128,1,128]{5,2,1,3,0,4:T(2,128)(2,1)S(1)} %bitcast.319) | data formatting | bytes 8388608 | tf_op jit(solution)/shard_map/reshape | solution.py:182
  311.0 6.0 %all-to-all-start.8 = ((bf16[2,32,2,128,1,128]{5,2,3,0,4,1:T(2,128)(2,1)}), bf16[2,32,2,128,1,128]{5,2,3,0,4,1:T(2,128)(2,1)}, u32[]{:S(2)}, u32[]{:S(2)}) async-start(bf16[2,32,2,128,1,128]{5,2,3,0,4,1:T(2,128)(2,1)} %copy.190), calls=%async_computation.8 | async-start | bytes 8388608 | tf_op jit(solution)/shard_map/all_to_all | solution.py:181
  317.4 1.3 fusion.17
  319.7 1.5 fusion.22
  322.4 3.3 collective-permute-start.2
  325.8 1.4 collective-permute-start.3
  329.4 1.1 fusion.12
  330.5 1.1 fusion.13
  331.7 4.2 collective-permute-done.3
  336.7 3.0 scatter-add.11
  339.7 68.0 %all-to-all-done.8 = bf16[2,32,2,128,1,128]{5,2,3,0,4,1:T(2,128)(2,1)} async-done(((bf16[2,32,2,128,1,128]{5,2,3,0,4,1:T(2,128)(2,1)}), bf16[2,32,2,128,1,128]{5,2,3,0,4,1:T(2,128)(2,1)}, u32[]{:S(2)}, u32[]{:S(2)}) %all-to-all-start.8) | async-done | bytes 4194336 | tf_op jit(solution)/shard_map/all_to_all | solution.py:181
  407.7 14.6 %all-to-all-start.7 = ((bf16[16,64,128]{2,1,0:T(8,128)(2,1)}), bf16[16,64,128]{2,1,0:T(8,128)(2,1)S(1)}, u32[]{:S(2)}, u32[]{:S(2)}) async-start(bf16[16,64,128]{2,1,0:T(8,128)(2,1)} %bitcast.67), calls=%async_computation.7 | async-start | bytes 524288 | tf_op jit(solution)/shard_map/all_to_all | solution.py:210
  422.3 65.6 %all-reduce.8.cloned.1.call-done = bf16[2,256,1,128]{3,1,2,0:T(8,128)(2,1)} async-done(((bf16[2,256,1,128]{3,1,2,0:T(8,128)(2,1)}), bf16[2,256,1,128]{3,1,2,0:T(8,128)(2,1)}) %all-reduce.8.cloned.1.call-update) | async-done | bytes 131088 | tf_op jit(solution)/shard_map/psum | solution.py:153
  487.9 0.9 convert_select_fusion
  489.1 9.0 %copy.191 = bf16[2,32,2,128,1,128]{5,2,1,3,0,4:T(2,128)(2,1)} copy(bf16[2,32,2,128,1,128]{5,2,3,0,4,1:T(2,128)(2,1)} %all-to-all-done.8) | data formatting | bytes 8388608 | tf_op jit(solution)/shard_map/all_to_all | solution.py:181
  498.1 11.5 %all-to-all-start.5 = ((bf16[16,64,128]{2,1,0:T(8,128)(2,1)}), bf16[16,64,128]{2,1,0:T(8,128)(2,1)S(1)}, u32[]{:S(2)}, u32[]{:S(2)}) async-start(bf16[16,64,128]{2,1,0:T(8,128)(2,1)} %bitcast.45), calls=%async_computation.5 | async-start | bytes 524288 | tf_op jit(solution)/shard_map/all_to_all | solution.py:203
  509.7 2.8 fusion.7
  512.5 0.7 copy.194
  513.3 8.1 %all-to-all-done.5 = bf16[16,64,128]{2,1,0:T(8,128)(2,1)S(1)} async-done(((bf16[16,64,128]{2,1,0:T(8,128)(2,1)}), bf16[16,64,128]{2,1,0:T(8,128)(2,1)S(1)}, u32[]{:S(2)}, u32[]{:S(2)}) %all-to-all-start.5) | async-done | bytes 262176 | tf_op jit(solution)/shard_map/all_to_all | solution.py:203
  521.4 3.4 all-to-all-start.10
  524.8 0.7 copy_bitcast_fusion.5
  525.5 0.7 copy.192
  526.3 9.6 %all-to-all-done.10 = bf16[16,64,128]{2,1,0:T(8,128)(2,1)S(1)} async-done(((bf16[16,64,128]{2,1,0:T(8,128)(2,1)}), bf16[16,64,128]{2,1,0:T(8,128)(2,1)S(1)}, u32[]{:S(2)}, u32[]{:S(2)}) %all-to-all-start.10) | async-done | bytes 262176 | tf_op jit(solution)/shard_map/all_to_all | solution.py:218
  535.9 3.4 all-to-all-start.9
  539.4 0.7 copy_bitcast_fusion.6
  540.1 0.7 copy_bitcast_fusion.3
  540.8 10.2 %all-to-all-done.9 = bf16[16,64,128]{2,1,0:T(8,128)(2,1)S(1)} async-done(((bf16[16,64,128]{2,1,0:T(8,128)(2,1)}), bf16[16,64,128]{2,1,0:T(8,128)(2,1)S(1)}, u32[]{:S(2)}, u32[]{:S(2)}) %all-to-all-start.9) | async-done | bytes 262176 | tf_op jit(solution)/shard_map/all_to_all | solution.py:217
  551.1 0.7 copy_bitcast_fusion.4
  (108 shorter events, 14.6 us)
Async XLA Ops:
  7.2 15.8 %copy-start = (bf16[64,2048]{1,0:T(8,128)(2,1)S(1)}, bf16[64,2048]{1,0:T(8,128)(2,1)}, u32[]{:S(2)}) copy-start(bf16[64,2048]{1,0:T(8,128)(2,1)} %param.11) | copy-start | bytes 786436
  7.2 48.7 %copy-start.17 = (bf16[64,2048]{1,0:T(8,128)(2,1)S(1)}, bf16[64,2048]{1,0:T(8,128)(2,1)}, u32[]{:S(2)}) copy-start(bf16[64,2048]{1,0:T(8,128)(2,1)} %param.13) | copy-start | bytes 786436
  7.2 49.4 %copy-start.18 = (bf16[64,2048]{1,0:T(8,128)(2,1)S(1)}, bf16[64,2048]{1,0:T(8,128)(2,1)}, u32[]{:S(2)}) copy-start(bf16[64,2048]{1,0:T(8,128)(2,1)} %param.14) | copy-start | bytes 786436
  9.3 22.2 %all-to-all-start.3 = ((s32[32,1,2]{2,1,0:T(1,128)}), s32[32,1,2]{2,1,0:T(1,128)S(1)}, u32[]{:S(2)}, u32[]{:S(2)}) async-start(s32[32,1,2]{2,1,0:T(1,128)} %bitcast.20), calls=%async_computation.3 | async-start | bytes 32768 | tf_op jit(solution)/shard_map/all_to_all | solution.py:125
  31.5 20.9 %all-to-all-start.2 = ((bf16[64,16,128]{2,0,1:T(8,128)(2,1)}), bf16[64,16,128]{2,0,1:T(8,128)(2,1)S(1)}, u32[]{:S(2)}, u32[]{:S(2)}) async-start(bf16[64,16,128]{2,0,1:T(8,128)(2,1)} %copy_bitcast_fusion.8), calls=%async_computation.2 | async-start | bytes 524288 | tf_op jit(solution)/shard_map/all_to_all | solution.py:104
  52.4 14.6 %all-to-all-start = ((bf16[64,16,128]{2,0,1:T(8,128)(2,1)}), bf16[64,16,128]{2,0,1:T(8,128)(2,1)S(1)}, u32[]{:S(2)}, u32[]{:S(2)}) async-start(bf16[64,16,128]{2,0,1:T(8,128)(2,1)} %copy_bitcast_fusion.10), calls=%async_computation | async-start | bytes 524288 | tf_op jit(solution)/shard_map/all_to_all | solution.py:105
  67.0 15.1 %all-to-all-start.1 = ((bf16[64,16,128]{2,0,1:T(8,128)(2,1)}), bf16[64,16,128]{2,0,1:T(8,128)(2,1)S(1)}, u32[]{:S(2)}, u32[]{:S(2)}) async-start(bf16[64,16,128]{2,0,1:T(8,128)(2,1)} %copy_bitcast_fusion.9), calls=%async_computation.1 | async-start | bytes 524288 | tf_op jit(solution)/shard_map/all_to_all | solution.py:106
  82.1 14.5 %all-to-all-start.6 = ((bf16[64,16,128]{2,0,1:T(8,128)(2,1)}), bf16[64,16,128]{2,0,1:T(8,128)(2,1)S(1)}, u32[]{:S(2)}, u32[]{:S(2)}) async-start(bf16[64,16,128]{2,0,1:T(8,128)(2,1)} %copy_bitcast_fusion.7), calls=%async_computation.6 | async-start | bytes 524288 | tf_op jit(solution)/shard_map/all_to_all | solution.py:107
  96.7 183.7 %all-to-all-start.4 = ((bf16[2,32,2,128,1,128]{5,3,2,0,4,1:T(8,128)(2,1)}), bf16[2,32,2,128,1,128]{5,3,2,0,4,1:T(8,128)(2,1)}, u32[]{:S(2)}, u32[]{:S(2)}) async-start(bf16[2,32,2,128,1,128]{5,3,2,0,4,1:T(8,128)(2,1)} %copy.170), calls=%async_computation.4 | async-start | bytes 8388608 | tf_op jit(solution)/shard_map/all_to_all | solution.py:134
  101.5 175.6 %all-reduce.6.cloned.1.call-start = ((), (), s32[]{:S(2)}) async-start(), calls=%async_computation.11 | async-start | bytes 262144 | tf_op jit(solution)/shard_map/psum | solution.py:30
  101.9 12.5 %collective-permute-start = (bf16[2,128,128]{2,1,0:T(8,128)(2,1)S(1)}, bf16[2,128,128]{2,1,0:T(8,128)(2,1)S(1)}, u32[]{:S(2)}, u32[]{:S(2)}) collective-permute-start(bf16[2,128,128]{2,1,0:T(8,128)(2,1)S(1)} %get-tuple-element.58), channel_id=1, source_target_pairs={{0,1},{1,2},{2,3},{3,4},{4,5},{5,6},{6,7},{7,8},{8,9},{9,10},{10,1... | collective-permute-start | bytes 196616 | tf_op jit(solution)/shard_map/ppermute | solution.py:19
  104.9 9.6 %collective-permute-start.1 = (bf16[2,128,128]{2,1,0:T(8,128)(2,1)S(1)}, bf16[2,128,128]{2,1,0:T(8,128)(2,1)S(1)}, u32[]{:S(2)}, u32[]{:S(2)}) collective-permute-start(bf16[2,128,128]{2,1,0:T(8,128)(2,1)S(1)} %get-tuple-element.59), channel_id=1, source_target_pairs={{1,0},{2,1},{3,2},{4,3},{5,4},{6,5},{7,6},{8,7},{9,8},{10,9},{11,1... | collective-permute-start | bytes 196616 | tf_op jit(solution)/shard_map/ppermute | solution.py:21
  115.0 1.1 copy-start.6
  291.1 1.8 copy-start.10
  291.1 3.3 copy-start.12
  294.4 1.4 copy-start.8
  294.4 1.7 copy-start.9
  300.4 1.4 copy-start.2
  300.4 2.0 copy-start.4
  311.0 7.8 %copy-start.3 = (bf16[8,1,128,1024]{2,3,0,1:T(8,128)(2,1)S(1)}, bf16[8,1,128,1024]{2,3,0,1:T(8,128)(2,1)}, u32[]{:S(2)}) copy-start(bf16[8,1,128,1024]{2,3,0,1:T(8,128)(2,1)} %copy-done.2) | copy-start | bytes 6291460
  311.0 96.8 %all-to-all-start.8 = ((bf16[2,32,2,128,1,128]{5,2,3,0,4,1:T(2,128)(2,1)}), bf16[2,32,2,128,1,128]{5,2,3,0,4,1:T(2,128)(2,1)}, u32[]{:S(2)}, u32[]{:S(2)}) async-start(bf16[2,32,2,128,1,128]{5,2,3,0,4,1:T(2,128)(2,1)} %copy.190), calls=%async_computation.8 | async-start | bytes 8388608 | tf_op jit(solution)/shard_map/all_to_all | solution.py:181
  317.0 170.9 %all-reduce.8.cloned.1.call-start = ((), (), s32[]{:S(2)}) async-start(), calls=%async_computation.12 | async-start | bytes 262144 | tf_op jit(solution)/shard_map/psum | solution.py:153
  322.1 5.1 copy-start.16
  322.4 5.6 copy-start.14
  322.4 4.9 copy-start.5
  322.4 5.6 copy-start.13
  322.4 9.2 %collective-permute-start.2 = (bf16[2,128,1,128]{3,1,0,2:T(8,128)(2,1)S(1)}, bf16[2,128,1,128]{3,1,0,2:T(8,128)(2,1)S(1)}, u32[]{:S(2)}, u32[]{:S(2)}) collective-permute-start(bf16[2,128,1,128]{3,1,0,2:T(8,128)(2,1)S(1)} %get-tuple-element.49), channel_id=1, source_target_pairs={{0,1},{1,2},{2,3},{3,4},{4,5},{5,6},{6,7},{7,8},{8,9},{9,10},{10,1... | collective-permute-start | bytes 196616 | tf_op jit(solution)/shard_map/ppermute | solution.py:19
  325.8 2.6 copy-start.11
  325.8 10.1 %collective-permute-start.3 = (bf16[2,128,1,128]{3,1,0,2:T(8,128)(2,1)S(1)}, bf16[2,128,1,128]{3,1,0,2:T(8,128)(2,1)S(1)}, u32[]{:S(2)}, u32[]{:S(2)}) collective-permute-start(bf16[2,128,1,128]{3,1,0,2:T(8,128)(2,1)S(1)} %get-tuple-element.50), channel_id=1, source_target_pairs={{1,0},{2,1},{3,2},{4,3},{5,4},{6,5},{7,6},{8,7},{9,8},{10,9},{11,1... | collective-permute-start | bytes 196616 | tf_op jit(solution)/shard_map/ppermute | solution.py:21
  327.9 1.4 copy-start.7
  330.5 5.4 copy-start.15
  330.5 5.4 slice-start
  407.7 90.4 %all-to-all-start.7 = ((bf16[16,64,128]{2,1,0:T(8,128)(2,1)}), bf16[16,64,128]{2,1,0:T(8,128)(2,1)S(1)}, u32[]{:S(2)}, u32[]{:S(2)}) async-start(bf16[16,64,128]{2,1,0:T(8,128)(2,1)} %bitcast.67), calls=%async_computation.7 | async-start | bytes 524288 | tf_op jit(solution)/shard_map/all_to_all | solution.py:210
  498.1 23.2 %all-to-all-start.5 = ((bf16[16,64,128]{2,1,0:T(8,128)(2,1)}), bf16[16,64,128]{2,1,0:T(8,128)(2,1)S(1)}, u32[]{:S(2)}, u32[]{:S(2)}) async-start(bf16[16,64,128]{2,1,0:T(8,128)(2,1)} %bitcast.45), calls=%async_computation.5 | async-start | bytes 524288 | tf_op jit(solution)/shard_map/all_to_all | solution.py:203
  512.5 39.3 %copy-start.1 = (bf16[64,2048]{1,0:T(8,128)(2,1)S(1)}, bf16[64,2048]{1,0:T(8,128)(2,1)}, u32[]{:S(2)}) copy-start(bf16[64,2048]{1,0:T(8,128)(2,1)} %param.11) | copy-start | bytes 786436
  521.4 14.6 %all-to-all-start.10 = ((bf16[16,64,128]{2,1,0:T(8,128)(2,1)}), bf16[16,64,128]{2,1,0:T(8,128)(2,1)S(1)}, u32[]{:S(2)}, u32[]{:S(2)}) async-start(bf16[16,64,128]{2,1,0:T(8,128)(2,1)} %bitcast.126), calls=%async_computation.10 | async-start | bytes 524288 | tf_op jit(solution)/shard_map/all_to_all | solution.py:218
  535.9 15.1 %all-to-all-start.9 = ((bf16[16,64,128]{2,1,0:T(8,128)(2,1)}), bf16[16,64,128]{2,1,0:T(8,128)(2,1)S(1)}, u32[]{:S(2)}, u32[]{:S(2)}) async-start(bf16[16,64,128]{2,1,0:T(8,128)(2,1)} %bitcast.124), calls=%async_computation.9 | async-start | bytes 524288 | tf_op jit(solution)/shard_map/all_to_all | solution.py:217
Sparse Core Ops, SparseCore 0:
  107.2 169.8 all-reduce.5
  322.3 165.5 all-reduce.7
where the time goes:
time: 560 us; the launch traced here: 559 us
  waiting for transfers between devices  372 us (66%)
  starting transfers between devices  86.6 us (15%)
  local copies, waits for them, and re-layouts  53 us (9%)
  matrix products  18.1 us (3%)
  between operations  14.7 us (3%)
  other arithmetic  13.9 us (2%)
    psum x1, waiting for transfers between devices, broadcast(): return lax.psum(kept, axis)  159 us
    all_to_all x1, waiting for transfers between devices, shards(): lax.all_to_all(outgoing.reshape(2, groups, capacity, BLK, head_count, HD)...  68 us
    psum x1, waiting for transfers between devices, shards(): lax.psum(jnp.stack([key_global, value_global]).astype(jnp.bfloat16), 'seq')  65.6 us
    all_to_all x1, starting transfers between devices, shards(): lax.all_to_all(grad_q.reshape(group_tokens, head_count * HD), 'head', spl...  14.6 us
    all_to_all x1, starting transfers between devices, shards(): lax.all_to_all(request_table(random_blocks, query_count, groups, capacity...  13.7 us
    all_to_all x1, waiting for transfers between devices, shards(): lax.all_to_all(values, 'head', split_axis=1, concat_axis=0, tiled=True)  11.6 us
    all_to_all x1, starting transfers between devices, shards(): lax.all_to_all(attended.reshape(group_tokens, head_count * HD), 'head', s...  11.5 us
  transfers between devices with their start and end apart: 17, of which 13 were waited for; matrix products, arithmetic and copies ran while one was open for 9% of the time, Pallas kernels for 0%

commit v1 on v0

--- a/solution.py
+++ b/solution.py
@@ -150,9 +150,9 @@
     grad_q = weigh_keys(grad_score, global_kv[0], window_kv[0], remote_kv[0]).astype(jnp.bfloat16)
     key_global, key_window, key_random = key_terms(grad_score, query_blocks)
     value_global, value_window, value_random = key_terms(weights, grad_blocks)
-    global_sum = lax.psum(jnp.stack([key_global, value_global]).astype(jnp.bfloat16), "seq").astype(
-        jnp.float32
-    )
+    global_sum = jnp.sum(
+        lax.all_gather(jnp.stack([key_global, value_global]).astype(jnp.bfloat16), "seq"), axis=0
+    ).astype(jnp.float32)
     window_grad = jnp.stack([key_window, value_window]).reshape(
         2, query_count, 3, BLK, head_count, HD
     )

time: 560 us -> 506 us (0.904)
  waiting for transfers between devices: 372 us -> 309 us
  starting transfers between devices: 86.6 us -> 93.5 us
    psum x1 -> x0, waiting for transfers between devices: 65.6 us -> none  [shards(): lax.psum(jnp.stack([key_global, value_global]).astype(jnp.bfloat16), 'seq')]
    all_to_all x1, starting transfers between devices: 14.6 us -> 25.9 us  [shards(): lax.all_to_all(grad_q.reshape(group_tokens, head_count * HD), 'head', spl...]
  transfers between devices with their start and end apart: 17 -> 17, of which waited for: 13 -> 12; matrix products, arithmetic and copies ran while one was open for 9% -> 10% of each run, Pallas kernels for 0% -> 0%
where the time goes in v1:
time: 506 us; the launch traced here: 503 us
  waiting for transfers between devices  309 us (61%)
  starting transfers between devices  93.5 us (18%)
  local copies, waits for them, and re-layouts  52.9 us (10%)
  matrix products  17.1 us (3%)
  other arithmetic  15.8 us (3%)
  between operations  14.8 us (3%)
    psum x1, waiting for transfers between devices, broadcast(): return lax.psum(kept, axis)  159 us
    all_to_all x1, waiting for transfers between devices, shards(): lax.all_to_all(outgoing.reshape(2, groups, capacity, BLK, head_count, HD)...  69.6 us
    all_to_all x1, starting transfers between devices, shards(): lax.all_to_all(grad_q.reshape(group_tokens, head_count * HD), 'head', spl...  25.9 us
    all_to_all x1, starting transfers between devices, shards(): lax.all_to_all(request_table(random_blocks, query_count, groups, capacity...  13.7 us
    all_to_all x1, waiting for transfers between devices, shards(): lax.all_to_all(values, 'head', split_axis=1, concat_axis=0, tiled=True)  11.6 us
    all_to_all x1, waiting for transfers between devices, shards(): lax.all_to_all(grad_k, 'head', split_axis=0, concat_axis=1, tiled=True)  10.2 us
  transfers between devices with their start and end apart: 17, of which 12 were waited for; matrix products, arithmetic and copies ran while one was open for 10% of the time, Pallas kernels for 0%

profile of v1, /device:TPU:1, one launch (start us, length us, event | category | flops | bytes accessed | tf_op | source)
XLA Modules:
  0.0 503.0 jit_solution(3612377534694347022)
XLA Ops:
  7.2 0.8 copy.164
  8.5 0.7 all_to_all.121
  9.3 13.7 %all-to-all-start.3 = ((s32[32,1,2]{2,1,0:T(1,128)}), s32[32,1,2]{2,1,0:T(1,128)S(1)}, u32[]{:S(2)}, u32[]{:S(2)}) async-start(s32[32,1,2]{2,1,0:T(1,128)} %bitcast.20), calls=%async_computation.3 | async-start | bytes 32768 | tf_op jit(solution)/shard_map/all_to_all | solution.py:125
  23.0 0.8 copy_bitcast_fusion.8
  23.8 7.7 %all-to-all-done.3 = s32[32,1,2]{2,1,0:T(1,128)S(1)} async-done(((s32[32,1,2]{2,1,0:T(1,128)}), s32[32,1,2]{2,1,0:T(1,128)S(1)}, u32[]{:S(2)}, u32[]{:S(2)}) %all-to-all-start.3) | async-done | bytes 288 | tf_op jit(solution)/shard_map/all_to_all | solution.py:125
  31.5 9.2 %all-to-all-start.2 = ((bf16[64,16,128]{2,0,1:T(8,128)(2,1)}), bf16[64,16,128]{2,0,1:T(8,128)(2,1)S(1)}, u32[]{:S(2)}, u32[]{:S(2)}) async-start(bf16[64,16,128]{2,0,1:T(8,128)(2,1)} %copy_bitcast_fusion.8), calls=%async_computation.2 | async-start | bytes 524288 | tf_op jit(solution)/shard_map/all_to_all | solution.py:104
  40.7 1.7 copy_bitcast_fusion.10
  42.4 10.0 %all-to-all-done.2 = bf16[64,16,128]{2,0,1:T(8,128)(2,1)S(1)} async-done(((bf16[64,16,128]{2,0,1:T(8,128)(2,1)}), bf16[64,16,128]{2,0,1:T(8,128)(2,1)S(1)}, u32[]{:S(2)}, u32[]{:S(2)}) %all-to-all-start.2) | async-done | bytes 262176 | tf_op jit(solution)/shard_map/all_to_all | solution.py:104
  52.4 3.4 all-to-all-start
  55.9 0.8 copy_bitcast_fusion.9
  56.6 0.8 copy_bitcast_fusion.7
  57.9 0.7 reduce.16
  58.8 8.2 %all-to-all-done = bf16[64,16,128]{2,0,1:T(8,128)(2,1)S(1)} async-done(((bf16[64,16,128]{2,0,1:T(8,128)(2,1)}), bf16[64,16,128]{2,0,1:T(8,128)(2,1)S(1)}, u32[]{:S(2)}, u32[]{:S(2)}) %all-to-all-start) | async-done | bytes 262176 | tf_op jit(solution)/shard_map/all_to_all | solution.py:105
  67.0 3.4 all-to-all-start.1
  70.6 11.6 %all-to-all-done.1 = bf16[64,16,128]{2,0,1:T(8,128)(2,1)S(1)} async-done(((bf16[64,16,128]{2,0,1:T(8,128)(2,1)}), bf16[64,16,128]{2,0,1:T(8,128)(2,1)S(1)}, u32[]{:S(2)}, u32[]{:S(2)}) %all-to-all-start.1) | async-done | bytes 262176 | tf_op jit(solution)/shard_map/all_to_all | solution.py:106
  82.1 3.4 all-to-all-start.6
  85.6 3.0 gather_fusion
  88.7 2.7 copy.168
  91.9 2.5 copy.169
  94.4 2.3 all-to-all-done.6
  96.7 4.9 all-to-all-start.4
  101.9 3.0 collective-permute-start
  104.9 1.5 collective-permute-start.1
  107.0 7.4 %collective-permute-done = bf16[2,128,128]{2,1,0:T(8,128)(2,1)S(1)} collective-permute-done((bf16[2,128,128]{2,1,0:T(8,128)(2,1)S(1)}, bf16[2,128,128]{2,1,0:T(8,128)(2,1)S(1)}, u32[]{:S(2)}, u32[]{:S(2)}) %collective-permute-start) | collective-permute-done | bytes 65568 | tf_op jit(solution)/shard_map/ppermute | solution.py:19
  115.4 0.8 copy-done.6
  116.2 1.5 convolution_bitcast_fusion.1
  117.7 159.4 %all-reduce.5.cloned.1.call-done = bf16[2,256,1,128]{3,1,2,0:T(8,128)(2,1)} async-done(((bf16[2,256,1,128]{3,1,2,0:T(8,128)(2,1)}), bf16[2,256,1,128]{3,1,2,0:T(8,128)(2,1)}) %all-reduce.5.cloned.1.call-update) | async-done | bytes 131088 | tf_op jit(solution)/shard_map/psum | solution.py:30
  277.1 1.1 convolution_bitcast_fusion.6
  278.2 2.1 convolution_bitcast_fusion.5
  280.4 4.8 copy.170
  285.2 4.2 gather_fusion.1
  289.3 1.6 bitcast_select_fusion
  291.5 1.4 fusion.20
  292.9 1.5 fusion.2
  294.8 1.0 copy-done.8
  296.1 1.9 multiply_reduce_fusion
  298.0 2.3 multiply_convert_fusion
  303.4 1.4 convolution_convert_fusion
  304.7 6.7 %copy.189 = bf16[2,32,2,128,1,128]{5,2,3,0,4,1:T(2,128)(2,1)} copy(bf16[2,32,2,128,1,128]{5,2,1,3,0,4:T(2,128)(2,1)S(1)} %bitcast.319) | data formatting | bytes 8388608 | tf_op jit(solution)/shard_map/reshape | solution.py:182
  311.4 5.9 %all-to-all-start.8 = ((bf16[2,32,2,128,1,128]{5,2,3,0,4,1:T(2,128)(2,1)}), bf16[2,32,2,128,1,128]{5,2,3,0,4,1:T(2,128)(2,1)}, u32[]{:S(2)}, u32[]{:S(2)}) async-start(bf16[2,32,2,128,1,128]{5,2,3,0,4,1:T(2,128)(2,1)} %copy.189), calls=%async_computation.8 | async-start | bytes 8388608 | tf_op jit(solution)/shard_map/all_to_all | solution.py:181
  318.4 1.5 fusion.22
  321.1 3.3 collective-permute-start.2
  324.5 1.4 collective-permute-start.3
  328.1 1.1 fusion.12
  329.2 1.1 fusion.13
  330.4 4.9 collective-permute-done.3
  336.1 3.0 scatter-add.11
  339.0 69.6 %all-to-all-done.8 = bf16[2,32,2,128,1,128]{5,2,3,0,4,1:T(2,128)(2,1)} async-done(((bf16[2,32,2,128,1,128]{5,2,3,0,4,1:T(2,128)(2,1)}), bf16[2,32,2,128,1,128]{5,2,3,0,4,1:T(2,128)(2,1)}, u32[]{:S(2)}, u32[]{:S(2)}) %all-to-all-start.8) | async-done | bytes 4194336 | tf_op jit(solution)/shard_map/all_to_all | solution.py:181
  408.6 25.9 %all-to-all-start.7 = ((bf16[16,64,128]{2,1,0:T(8,128)(2,1)}), bf16[16,64,128]{2,1,0:T(8,128)(2,1)S(1)}, u32[]{:S(2)}, u32[]{:S(2)}) async-start(bf16[16,64,128]{2,1,0:T(8,128)(2,1)} %bitcast.67), calls=%async_computation.7 | async-start | bytes 524288 | tf_op jit(solution)/shard_map/all_to_all | solution.py:210
  434.5 9.0 %copy.190 = bf16[2,32,2,128,1,128]{5,2,1,3,0,4:T(2,128)(2,1)} copy(bf16[2,32,2,128,1,128]{5,2,3,0,4,1:T(2,128)(2,1)} %all-to-all-done.8) | data formatting | bytes 8388608 | tf_op jit(solution)/shard_map/all_to_all | solution.py:181
  443.6 2.8 reduce_sum.59
  446.7 7.2 %all-to-all-start.5 = ((bf16[16,64,128]{2,1,0:T(8,128)(2,1)}), bf16[16,64,128]{2,1,0:T(8,128)(2,1)S(1)}, u32[]{:S(2)}, u32[]{:S(2)}) async-start(bf16[16,64,128]{2,1,0:T(8,128)(2,1)} %bitcast.45), calls=%async_computation.5 | async-start | bytes 524288 | tf_op jit(solution)/shard_map/all_to_all | solution.py:203
  454.0 2.8 fusion.7
  456.9 0.7 copy.193
  457.6 8.1 %all-to-all-done.5 = bf16[16,64,128]{2,1,0:T(8,128)(2,1)S(1)} async-done(((bf16[16,64,128]{2,1,0:T(8,128)(2,1)}), bf16[16,64,128]{2,1,0:T(8,128)(2,1)S(1)}, u32[]{:S(2)}, u32[]{:S(2)}) %all-to-all-start.5) | async-done | bytes 262176 | tf_op jit(solution)/shard_map/all_to_all | solution.py:203
  465.7 3.4 all-to-all-start.10
  469.1 0.7 copy_bitcast_fusion.5
  469.9 0.7 copy.191
  470.6 9.6 %all-to-all-done.10 = bf16[16,64,128]{2,1,0:T(8,128)(2,1)S(1)} async-done(((bf16[16,64,128]{2,1,0:T(8,128)(2,1)}), bf16[16,64,128]{2,1,0:T(8,128)(2,1)S(1)}, u32[]{:S(2)}, u32[]{:S(2)}) %all-to-all-start.10) | async-done | bytes 262176 | tf_op jit(solution)/shard_map/all_to_all | solution.py:218
  480.2 3.4 all-to-all-start.9
  483.7 0.7 copy_bitcast_fusion.6
  484.4 0.7 copy_bitcast_fusion.3
  485.2 10.2 %all-to-all-done.9 = bf16[16,64,128]{2,1,0:T(8,128)(2,1)S(1)} async-done(((bf16[16,64,128]{2,1,0:T(8,128)(2,1)}), bf16[16,64,128]{2,1,0:T(8,128)(2,1)S(1)}, u32[]{:S(2)}, u32[]{:S(2)}) %all-to-all-start.9) | async-done | bytes 262176 | tf_op jit(solution)/shard_map/all_to_all | solution.py:217
  495.4 0.7 copy_bitcast_fusion.4
  (109 shorter events, 13.4 us)
Async XLA Ops:
  7.2 15.8 %copy-start = (bf16[64,2048]{1,0:T(8,128)(2,1)S(1)}, bf16[64,2048]{1,0:T(8,128)(2,1)}, u32[]{:S(2)}) copy-start(bf16[64,2048]{1,0:T(8,128)(2,1)} %param.11) | copy-start | bytes 786436
  7.2 48.7 %copy-start.17 = (bf16[64,2048]{1,0:T(8,128)(2,1)S(1)}, bf16[64,2048]{1,0:T(8,128)(2,1)}, u32[]{:S(2)}) copy-start(bf16[64,2048]{1,0:T(8,128)(2,1)} %param.13) | copy-start | bytes 786436
  7.2 49.4 %copy-start.18 = (bf16[64,2048]{1,0:T(8,128)(2,1)S(1)}, bf16[64,2048]{1,0:T(8,128)(2,1)}, u32[]{:S(2)}) copy-start(bf16[64,2048]{1,0:T(8,128)(2,1)} %param.14) | copy-start | bytes 786436
  9.3 22.2 %all-to-all-start.3 = ((s32[32,1,2]{2,1,0:T(1,128)}), s32[32,1,2]{2,1,0:T(1,128)S(1)}, u32[]{:S(2)}, u32[]{:S(2)}) async-start(s32[32,1,2]{2,1,0:T(1,128)} %bitcast.20), calls=%async_computation.3 | async-start | bytes 32768 | tf_op jit(solution)/shard_map/all_to_all | solution.py:125
  31.5 20.9 %all-to-all-start.2 = ((bf16[64,16,128]{2,0,1:T(8,128)(2,1)}), bf16[64,16,128]{2,0,1:T(8,128)(2,1)S(1)}, u32[]{:S(2)}, u32[]{:S(2)}) async-start(bf16[64,16,128]{2,0,1:T(8,128)(2,1)} %copy_bitcast_fusion.8), calls=%async_computation.2 | async-start | bytes 524288 | tf_op jit(solution)/shard_map/all_to_all | solution.py:104
  52.4 14.6 %all-to-all-start = ((bf16[64,16,128]{2,0,1:T(8,128)(2,1)}), bf16[64,16,128]{2,0,1:T(8,128)(2,1)S(1)}, u32[]{:S(2)}, u32[]{:S(2)}) async-start(bf16[64,16,128]{2,0,1:T(8,128)(2,1)} %copy_bitcast_fusion.10), calls=%async_computation | async-start | bytes 524288 | tf_op jit(solution)/shard_map/all_to_all | solution.py:105
  67.0 15.1 %all-to-all-start.1 = ((bf16[64,16,128]{2,0,1:T(8,128)(2,1)}), bf16[64,16,128]{2,0,1:T(8,128)(2,1)S(1)}, u32[]{:S(2)}, u32[]{:S(2)}) async-start(bf16[64,16,128]{2,0,1:T(8,128)(2,1)} %copy_bitcast_fusion.9), calls=%async_computation.1 | async-start | bytes 524288 | tf_op jit(solution)/shard_map/all_to_all | solution.py:106
  82.1 14.5 %all-to-all-start.6 = ((bf16[64,16,128]{2,0,1:T(8,128)(2,1)}), bf16[64,16,128]{2,0,1:T(8,128)(2,1)S(1)}, u32[]{:S(2)}, u32[]{:S(2)}) async-start(bf16[64,16,128]{2,0,1:T(8,128)(2,1)} %copy_bitcast_fusion.7), calls=%async_computation.6 | async-start | bytes 524288 | tf_op jit(solution)/shard_map/all_to_all | solution.py:107
  96.7 183.7 %all-to-all-start.4 = ((bf16[2,32,2,128,1,128]{5,3,2,0,4,1:T(8,128)(2,1)}), bf16[2,32,2,128,1,128]{5,3,2,0,4,1:T(8,128)(2,1)}, u32[]{:S(2)}, u32[]{:S(2)}) async-start(bf16[2,32,2,128,1,128]{5,3,2,0,4,1:T(8,128)(2,1)} %copy.169), calls=%async_computation.4 | async-start | bytes 8388608 | tf_op jit(solution)/shard_map/all_to_all | solution.py:134
  101.5 175.6 %all-reduce.5.cloned.1.call-start = ((), (), s32[]{:S(2)}) async-start(), calls=%async_computation.11 | async-start | bytes 262144 | tf_op jit(solution)/shard_map/psum | solution.py:30
  101.9 12.5 %collective-permute-start = (bf16[2,128,128]{2,1,0:T(8,128)(2,1)S(1)}, bf16[2,128,128]{2,1,0:T(8,128)(2,1)S(1)}, u32[]{:S(2)}, u32[]{:S(2)}) collective-permute-start(bf16[2,128,128]{2,1,0:T(8,128)(2,1)S(1)} %get-tuple-element.58), channel_id=1, source_target_pairs={{0,1},{1,2},{2,3},{3,4},{4,5},{5,6},{6,7},{7,8},{8,9},{9,10},{10,1... | collective-permute-start | bytes 196616 | tf_op jit(solution)/shard_map/ppermute | solution.py:19
  104.9 9.6 %collective-permute-start.1 = (bf16[2,128,128]{2,1,0:T(8,128)(2,1)S(1)}, bf16[2,128,128]{2,1,0:T(8,128)(2,1)S(1)}, u32[]{:S(2)}, u32[]{:S(2)}) collective-permute-start(bf16[2,128,128]{2,1,0:T(8,128)(2,1)S(1)} %get-tuple-element.59), channel_id=1, source_target_pairs={{1,0},{2,1},{3,2},{4,3},{5,4},{6,5},{7,6},{8,7},{9,8},{10,9},{11,1... | collective-permute-start | bytes 196616 | tf_op jit(solution)/shard_map/ppermute | solution.py:21
  115.0 1.2 copy-start.6
  291.1 1.8 copy-start.10
  291.1 3.3 copy-start.12
  294.4 1.4 copy-start.8
  294.4 1.7 copy-start.9
  300.4 1.4 copy-start.2
  300.4 2.0 copy-start.4
  311.4 97.3 %all-to-all-start.8 = ((bf16[2,32,2,128,1,128]{5,2,3,0,4,1:T(2,128)(2,1)}), bf16[2,32,2,128,1,128]{5,2,3,0,4,1:T(2,128)(2,1)}, u32[]{:S(2)}, u32[]{:S(2)}) async-start(bf16[2,32,2,128,1,128]{5,2,3,0,4,1:T(2,128)(2,1)} %copy.189), calls=%async_computation.8 | async-start | bytes 8388608 | tf_op jit(solution)/shard_map/all_to_all | solution.py:181
  317.3 2.6 copy-start.3
  317.3 126.2 %all-gather.2.cloned.1.call-start = ((), (), s32[]{:S(2)}) async-start(), calls=%async_computation.12 | async-start | bytes 4325376 | tf_op jit(solution)/shard_map/all_gather | solution.py:154
  320.8 5.1 %copy-start.16 = (bf16[2,256,1,128]{3,1,2,0:T(8,128)(2,1)S(1)}, bf16[2,256,1,128]{3,1,2,0:T(8,128)(2,1)}, u32[]{:S(2)}) copy-start(bf16[2,256,1,128]{3,1,2,0:T(8,128)(2,1)} %all-reduce.5.cloned.1.call-done) | copy-start | bytes 393220
  321.0 5.6 %copy-start.14 = (f32[2,10,128,1,128]{4,2,0,3,1:T(8,128)}, f32[2,10,128,1,128]{4,2,0,3,1:T(8,128)S(1)}, u32[]{:S(2)}) copy-start(f32[2,10,128,1,128]{4,2,0,3,1:T(8,128)S(1)} %bitcast_add_fusion) | copy-start | bytes 3932164
  321.1 4.9 copy-start.5
  321.1 5.6 %copy-start.13 = (bf16[1,24,128,1,128]{4,2,0,1,3:T(8,128)(2,1)S(1)}, bf16[1,24,128,1,128]{4,2,0,1,3:T(8,128)(2,1)}, u32[]{:S(2)}) copy-start(bf16[1,24,128,1,128]{4,2,0,1,3:T(8,128)(2,1)} %copy-done.12) | copy-start | bytes 2359300
  321.1 9.2 %collective-permute-start.2 = (bf16[2,128,1,128]{3,1,0,2:T(8,128)(2,1)S(1)}, bf16[2,128,1,128]{3,1,0,2:T(8,128)(2,1)S(1)}, u32[]{:S(2)}, u32[]{:S(2)}) collective-permute-start(bf16[2,128,1,128]{3,1,0,2:T(8,128)(2,1)S(1)} %get-tuple-element.49), channel_id=1, source_target_pairs={{0,1},{1,2},{2,3},{3,4},{4,5},{5,6},{6,7},{7,8},{8,9},{9,10},{10,1... | collective-permute-start | bytes 196616 | tf_op jit(solution)/shard_map/ppermute | solution.py:19
  324.5 2.6 copy-start.11
  324.5 10.8 %collective-permute-start.3 = (bf16[2,128,1,128]{3,1,0,2:T(8,128)(2,1)S(1)}, bf16[2,128,1,128]{3,1,0,2:T(8,128)(2,1)S(1)}, u32[]{:S(2)}, u32[]{:S(2)}) collective-permute-start(bf16[2,128,1,128]{3,1,0,2:T(8,128)(2,1)S(1)} %get-tuple-element.50), channel_id=1, source_target_pairs={{1,0},{2,1},{3,2},{4,3},{5,4},{6,5},{7,6},{8,7},{9,8},{10,9},{11,1... | collective-permute-start | bytes 196616 | tf_op jit(solution)/shard_map/ppermute | solution.py:21
  326.7 1.4 copy-start.7
  329.2 6.0 %copy-start.15 = (f32[2,10,128,1,128]{4,2,0,3,1:T(8,128)S(1)}, f32[2,10,128,1,128]{4,2,0,3,1:T(8,128)}, u32[]{:S(2)}) copy-start(f32[2,10,128,1,128]{4,2,0,3,1:T(8,128)} %copy-done.14) | copy-start | bytes 3932164
  329.2 6.0 %slice-start = ((f32[2,10,128,1,128]{4,2,0,3,1:T(8,128)}), f32[2,8,128,1,128]{4,2,0,3,1:T(8,128)S(1)}, s32[]{:S(2)}) async-start(f32[2,10,128,1,128]{4,2,0,3,1:T(8,128)} %copy-done.14), calls=%async_computation.13 | async-start | bytes 2097152 | tf_op jit(solution)/shard_map/slice | solution.py:167
  408.6 38.1 %all-to-all-start.7 = ((bf16[16,64,128]{2,1,0:T(8,128)(2,1)}), bf16[16,64,128]{2,1,0:T(8,128)(2,1)S(1)}, u32[]{:S(2)}, u32[]{:S(2)}) async-start(bf16[16,64,128]{2,1,0:T(8,128)(2,1)} %bitcast.67), calls=%async_computation.7 | async-start | bytes 524288 | tf_op jit(solution)/shard_map/all_to_all | solution.py:210
  446.7 18.9 %all-to-all-start.5 = ((bf16[16,64,128]{2,1,0:T(8,128)(2,1)}), bf16[16,64,128]{2,1,0:T(8,128)(2,1)S(1)}, u32[]{:S(2)}, u32[]{:S(2)}) async-start(bf16[16,64,128]{2,1,0:T(8,128)(2,1)} %bitcast.45), calls=%async_computation.5 | async-start | bytes 524288 | tf_op jit(solution)/shard_map/all_to_all | solution.py:203
  456.9 39.3 %copy-start.1 = (bf16[64,2048]{1,0:T(8,128)(2,1)S(1)}, bf16[64,2048]{1,0:T(8,128)(2,1)}, u32[]{:S(2)}) copy-start(bf16[64,2048]{1,0:T(8,128)(2,1)} %param.11) | copy-start | bytes 786436
  465.7 14.6 %all-to-all-start.10 = ((bf16[16,64,128]{2,1,0:T(8,128)(2,1)}), bf16[16,64,128]{2,1,0:T(8,128)(2,1)S(1)}, u32[]{:S(2)}, u32[]{:S(2)}) async-start(bf16[16,64,128]{2,1,0:T(8,128)(2,1)} %bitcast.126), calls=%async_computation.10 | async-start | bytes 524288 | tf_op jit(solution)/shard_map/all_to_all | solution.py:218
  480.2 15.1 %all-to-all-start.9 = ((bf16[16,64,128]{2,1,0:T(8,128)(2,1)}), bf16[16,64,128]{2,1,0:T(8,128)(2,1)S(1)}, u32[]{:S(2)}, u32[]{:S(2)}) async-start(bf16[16,64,128]{2,1,0:T(8,128)(2,1)} %bitcast.124), calls=%async_computation.9 | async-start | bytes 524288 | tf_op jit(solution)/shard_map/all_to_all | solution.py:217
Sparse Core Ops, SparseCore 0:
  107.2 169.8 all-reduce.4
  322.4 116.7 all-gather.1
